TPU v7x, 256 devices: a whole 4x4x8 slice. The times are simulated.
256 devices in a mesh: rows: 32 (over y, z), grp: 8 (over x, core).
Axes of the slice: x: 4, y: 4, z: 8, core: 2. Of those that a mesh axis runs over, the one named last changes fastest.
Arguments:
- item_table: bfloat16 [507904, 128], P(('rows', 'grp'))
- histories: int32 [16384, 64], P(('rows', 'grp')), may hold values from 0 to 507903, as said below
- counts: int32 [16384], P(('rows', 'grp')), may hold values from 32 to 64
Outputs:
- user_vectors: float32 [16384, 128], P(('rows', 'grp'))
- item_rhs: float32 [507904, 128], P(('rows', 'grp'))
Inputs may be any that keep to these rules, and one draw needn't show every extreme that they name: `histories`: entry j of user u is used only if j < counts[u]. The used entries of the users of one device name items of one owner (rows o * 1984 to (o + 1) * 1984 - 1) at most 32 times, and in every draw some owner is named exactly 32 times by the used entries of every device.
All inputs are finite; a program needn't handle non-finite values.
Results may differ from a plain program's by a relative error of at most 0.0064.
Values may be sent and summed in bfloat16 or wider, within the bound.
No kernel may reach another device: no remote copies, remote signals or barrier semaphores. Data moves between devices by JAX's collectives and lax.ppermute only.
A program may use at most 64 MiB of HBM per device.

v0:
```python
import jax
import jax.numpy as jnp
from jax import lax
from jax.sharding import PartitionSpec as P

ITERS = 3
unobserved_weight = 25.0
ridge = 0.1


def on_device(item_table, histories, counts):
    row_count = lax.axis_size("rows")
    group_count = lax.axis_size("grp")
    devices = row_count * group_count
    table_rows, embed_width = item_table.shape
    user_count, history_length = histories.shape
    lookups = user_count * history_length
    capacity = max(4, 2 * lookups // devices)
    slots_total = devices * capacity
    local_gram = lax.dot_general(
        item_table, item_table, (((0,), (0,)), ((), ())), preferred_element_type=jnp.float32
    )
    gramian = lax.psum(local_gram, ("rows", "grp"))
    positions = lax.broadcasted_iota(jnp.int32, (user_count, history_length), 1)
    live = positions < counts[:, None]
    weights = live.astype(jnp.float32)
    flat_ids = histories.reshape(-1)
    owners = flat_ids // table_rows
    local_rows = flat_ids - owners * table_rows
    owner_key = jnp.where(live.reshape(-1), owners, devices)
    ordering = jnp.argsort(owner_key, stable=True)
    sorted_key = owner_key[ordering]
    starts = jnp.searchsorted(sorted_key, jnp.arange(devices + 1, dtype=jnp.int32), side="left")
    ranks = jnp.arange(lookups, dtype=jnp.int32) - starts[sorted_key]
    sorted_slots = jnp.where(sorted_key < devices, sorted_key * capacity + ranks, slots_total)
    slot_index = jnp.zeros((lookups,), jnp.int32).at[ordering].set(sorted_slots)
    requests = (
        jnp.full((slots_total,), table_rows, jnp.int32).at[slot_index].set(local_rows, mode="drop")
    )
    requests = requests.reshape(row_count, group_count, capacity)
    incoming = lax.all_to_all(
        lax.all_to_all(requests, "grp", split_axis=1, concat_axis=1, tiled=True),
        "rows",
        split_axis=0,
        concat_axis=0,
        tiled=True,
    )
    answered = item_table[jnp.minimum(incoming, table_rows - 1)]
    replies = lax.all_to_all(
        lax.all_to_all(answered, "grp", split_axis=1, concat_axis=1, tiled=True),
        "rows",
        split_axis=0,
        concat_axis=0,
        tiled=True,
    )
    reply_rows = replies.reshape(slots_total, embed_width)
    fetched = reply_rows[jnp.minimum(slot_index, slots_total - 1)].reshape(
        user_count, history_length, embed_width
    )
    narrow_weights = weights.astype(jnp.bfloat16)
    target = jnp.einsum("ul,ulk->uk", narrow_weights, fetched, preferred_element_type=jnp.float32)
    unseen_scale = unobserved_weight / (table_rows * devices)
    solution = jnp.zeros_like(target)
    residual = target
    direction = target
    norm_now = jnp.sum(residual * residual, axis=1)
    for iteration in range(ITERS):
        narrow = direction.astype(jnp.bfloat16)
        scores = jnp.einsum("ulk,uk->ul", fetched, narrow, preferred_element_type=jnp.float32)
        scores = (scores * weights).astype(jnp.bfloat16)
        returned = jnp.einsum("ulk,ul->uk", fetched, scores, preferred_element_type=jnp.float32)
        curved = jnp.dot(direction, gramian, precision=lax.Precision.HIGHEST)
        applied = unseen_scale * curved + returned + ridge * direction
        step_size = norm_now / jnp.sum(direction * applied, axis=1)
        solution = solution + step_size[:, None] * direction
        residual = residual - step_size[:, None] * applied
        norm_next = jnp.sum(residual * residual, axis=1)
        direction = residual + (norm_next / norm_now)[:, None] * direction
        norm_now = norm_next
    repeated = jnp.repeat(solution, history_length, axis=0)
    partials = (
        jnp.zeros((slots_total, embed_width), jnp.float32).at[slot_index].set(repeated, mode="drop")
    )
    partials = partials.reshape(row_count, group_count, capacity, embed_width)
    arrived = lax.all_to_all(
        lax.all_to_all(partials, "grp", split_axis=1, concat_axis=1, tiled=True),
        "rows",
        split_axis=0,
        concat_axis=0,
        tiled=True,
    )
    item_rhs = (
        jnp.zeros((table_rows, embed_width), jnp.float32)
        .at[incoming.reshape(-1)]
        .add(arrived.reshape(-1, embed_width), mode="drop")
    )
    return (solution, item_rhs)


def solution(mesh):
    return jax.shard_map(
        on_device,
        mesh=mesh,
        in_specs=(P(("rows", "grp"), None), P(("rows", "grp"), None), P(("rows", "grp"))),
        out_specs=(P(("rows", "grp"), None), P(("rows", "grp"), None)),
        check_vma=False,
    )
```

profile of v0, /device:TPU:2, one launch (start us, length us, event | category | flops | bytes accessed | tf_op | source)
XLA Modules:
  0.0 701.0 jit_solution(2141229603027904647)
XLA Ops:
  8.9 5.8 sort.17
  14.7 23.0 %gather_fusion.1 = s32[4096]{0:T(1024)S(1)} fusion(s32[4096]{0:T(1024)S(1)} %get-tuple-element.108, s32[4096]{0:T(1024)S(1)} %get-tuple-element.109), kind=kCustom, calls=%fused_computation.1 | custom fusion | bytes 49152 | tf_op jit(solution)/shard_map/gather | solution.py:32
  37.8 30.3 %while.24 = (s32[]{:T(128)}, u32[257]{0:T(512)S(1)}, u32[257]{0:T(512)S(1)}, s32[4096]{0:T(1024)S(1)}, s32[]{:T(128)}, /*index=5*/s32[]{:T(128)}, s32[]{}) while((s32[]{:T(128)}, u32[257]{0:T(512)S(1)}, u32[257]{0:T(512)S(1)}, s32[4096]{0:T(1024)S(1)}, s32[]{:T(128)}, /*index=5*/s32[]{:T(128)}, s32[]{}) %tuple.47), condition=%wide.region_2.3_spmd.clone, body=%wide.region_1.2_spmd.clone.sunk | while | flops 5654 | bytes 21159 | solution.py:33
  37.8 2.2 gather_fusion
  40.1 2.2 gather_fusion
  44.8 2.2 gather_fusion
  47.1 2.2 gather_fusion
  49.4 2.2 gather_fusion
  51.8 2.2 gather_fusion
  54.1 2.2 gather_fusion
  56.4 2.2 gather_fusion
  58.7 2.2 gather_fusion
  61.1 2.2 gather_fusion
  63.4 2.2 gather_fusion
  68.1 25.9 %gather_fusion.2 = s32[4096]{0:T(1024)S(1)} fusion(s32[257]{0:T(512)S(1)} %convert_element_type.36, s32[4096]{0:T(1024)S(1)} %broadcast_clamp_fusion.1), kind=kCustom, calls=%fused_computation.2 | custom fusion | bytes 49152 | tf_op jit(solution)/shard_map/gather | solution.py:34
  94.0 15.5 %scatter_custom_fusion = s32[4096]{0:T(1024)S(1)} fusion(s32[4096]{0:T(1024)S(1)} %get-tuple-element.110, s32[4096]{0:T(1024)S(1)} %add_select_fusion.1, s32[]{:T(128)} %constant.59.clone.1), kind=kCustom, calls=%fused_computation.85 | custom fusion | bytes 16388 | tf_op jit(solution)/shard_map/scatter | solution.py:36
  109.5 15.5 %scatter_custom_fusion.1 = s32[8192]{0:T(1024)S(1)} fusion(s32[4096]{0:T(1024)S(1)} %get-tuple-element.106, s32[4096]{0:T(1024)S(1)} %get-tuple-element.107, s32[]{:T(128)} %constant.58.clone.1), kind=kCustom, calls=%fused_computation.79 | custom fusion | bytes 32772 | tf_op jit(solution)/shard_map/scatter | solution.py:38
  125.3 8.6 %all_to_all.30 = s32[8,1,1024]{2,1,0:T(1,128)S(1)} all-to-all(s32[8,1,1024]{2,1,0:T(1,128)S(1)} %reshape.212), channel_id=1, replica_groups=mesh['rows'=32,'grp'=8] {'grp'}, dimensions={0} | all-to-all | bytes 65536 | tf_op jit(solution)/shard_map/all_to_all | solution.py:42
  135.5 21.2 %all_to_all.31 = s32[32,1,256]{2,1,0:T(1,128)S(1)} all-to-all(s32[32,1,256]{2,1,0:T(1,128)S(1)} %reshape.214), channel_id=1, replica_groups=mesh['rows'=32,'grp'=8] {'rows'}, dimensions={0} | all-to-all | bytes 65536 | tf_op jit(solution)/shard_map/all_to_all | solution.py:41
  157.7 24.0 %gather_fusion.3 = bf16[8192,128]{1,0:T(8,128)(2,1)S(1)} fusion(bf16[1984,128]{1,0:T(8,128)(2,1)S(1)} %copy-done, s32[8192]{0:T(1024)S(1)} %broadcast_clamp_fusion), kind=kCustom, calls=%fused_computation.3 | custom fusion | bytes 4227072 | tf_op jit(solution)/shard_map/gather | solution.py:48
  182.2 30.0 %all_to_all.32 = bf16[32,8,32,128]{3,2,0,1:T(8,128)(2,1)S(1)} all-to-all(bf16[32,8,32,128]{3,2,0,1:T(8,128)(2,1)S(1)} %copy.16), channel_id=1, replica_groups=mesh['rows'=32,'grp'=8] {'grp'}, dimensions={1} | all-to-all | bytes 4194304 | tf_op jit(solution)/shard_map/all_to_all | solution.py:50
  214.1 4.0 all-to-all-start.3
  219.3 49.0 %all-to-all-done.3 = bf16[32,8,32,128]{3,2,1,0:T(8,128)(2,1)S(1)} async-done(((bf16[32,8,32,128]{3,2,1,0:T(8,128)(2,1)}), bf16[32,8,32,128]{3,2,1,0:T(8,128)(2,1)S(1)}, u32[]{:S(2)}, u32[]{:S(2)}) %all-to-all-start.3) | async-done | bytes 2097184 | tf_op jit(solution)/shard_map/all_to_all | solution.py:49
  268.4 14.9 %gather_fusion.4 = bf16[4096,128]{1,0:T(8,128)(2,1)} fusion(bf16[8192,128]{1,0:T(8,128)(2,1)S(1)} %bitcast.60, s32[4096]{0:T(1024)S(1)} %get-tuple-element.105), kind=kCustom, calls=%fused_computation.4 | custom fusion | bytes 2113536 | tf_op jit(solution)/shard_map/gather | solution.py:57
  288.5 179.1 %all-reduce.2.cloned.1.call-done = f32[128,128]{1,0:T(8,128)} async-done(((f32[128,128]{1,0:T(8,128)}), f32[128,128]{1,0:T(8,128)}) %all-reduce.2.cloned.1.call-update) | async-done | bytes 65552 | tf_op jit(solution)/shard_map/psum | solution.py:23
  474.6 12.8 %scatter_custom_fusion.2 = f32[8192,128]{1,0:T(8,128)} fusion(s32[4096]{0:T(1024)S(1)} %get-tuple-element.106, f32[4096,128]{1,0:T(8,128)S(1)} %bitcast.63, f32[]{:T(128)} %constant.71.clone.1), kind=kCustom, calls=%fused_computation.15 | custom fusion | bytes 4194308 | tf_op jit(solution)/shard_map/scatter | solution.py:82
  487.4 2.8 copy.18
  490.2 53.3 %all_to_all.33 = f32[32,8,32,128]{3,2,0,1:T(8,128)S(1)} all-to-all(f32[32,8,32,128]{3,2,0,1:T(8,128)S(1)} %copy.18), channel_id=1, replica_groups=mesh['rows'=32,'grp'=8] {'grp'}, dimensions={1} | all-to-all | bytes 8388608 | tf_op jit(solution)/shard_map/all_to_all | solution.py:86
  543.5 2.6 copy.19
  546.1 6.1 all-to-all-start.5
  552.4 96.5 %all-to-all-done.5 = f32[32,8,32,128]{3,2,1,0:T(8,128)} async-done(((f32[32,8,32,128]{3,2,1,0:T(8,128)}), f32[32,8,32,128]{3,2,1,0:T(8,128)}, u32[]{:S(2)}, u32[]{:S(2)}) %all-to-all-start.5) | async-done | bytes 4194336 | tf_op jit(solution)/shard_map/all_to_all | solution.py:85
  648.8 45.3 %scatter_custom_fusion.3 = f32[1984,128]{1,0:T(8,128)} fusion(s32[8192]{0:T(1024)S(1)} %bitcast.84, f32[8192,128]{1,0:T(8,128)} %bitcast.29, f32[]{:T(128)} %constant.71.clone.1), kind=kCustom, calls=%fused_computation.28 | custom fusion | flops 1048576 | bytes 1016320 | tf_op jit(solution)/shard_map/scatter-add | solution.py:95
  (135 shorter events, 25.4 us)
Async XLA Ops:
  7.2 150.5 %copy-start = (bf16[1984,128]{1,0:T(8,128)(2,1)S(1)}, bf16[1984,128]{1,0:T(8,128)(2,1)}, u32[]{:S(2)}) copy-start(bf16[1984,128]{1,0:T(8,128)(2,1)} %param.5) | copy-start | bytes 1523716
  214.1 54.3 %all-to-all-start.3 = ((bf16[32,8,32,128]{3,2,1,0:T(8,128)(2,1)}), bf16[32,8,32,128]{3,2,1,0:T(8,128)(2,1)S(1)}, u32[]{:S(2)}, u32[]{:S(2)}) async-start(bf16[32,8,32,128]{3,2,1,0:T(8,128)(2,1)} %copy.17), calls=%async_computation.3 | async-start | bytes 4194304 | tf_op jit(solution)/shard_map/all_to_all | solution.py:49
  218.1 249.5 %all-reduce.2.cloned.1.call-start = ((), (), s32[]{:S(2)}) async-start(), calls=%async_computation.6 | async-start | bytes 131072 | tf_op jit(solution)/shard_map/psum | solution.py:23
  268.4 18.5 %copy-start.4 = (s32[64]{0:T(128)S(1)}, s32[64]{0:T(128)}, u32[]{:S(2)}) copy-start(s32[64]{0:T(128)} %param.7) | copy-start | bytes 772
  283.3 187.8 %copy-start.1 = (bf16[4096,128]{1,0:T(8,128)(2,1)S(1)}, bf16[4096,128]{1,0:T(8,128)(2,1)}, u32[]{:S(2)}) copy-start(bf16[4096,128]{1,0:T(8,128)(2,1)} %gather_fusion.4) | copy-start | bytes 3145732
  467.6 6.4 copy-start.2
  474.5 15.7 %copy-start.3 = (f32[64,128]{1,0:T(8,128)}, f32[64,128]{1,0:T(8,128)S(1)}, u32[]{:S(2)}) copy-start(f32[64,128]{1,0:T(8,128)S(1)} %multiply_add_fusion) | copy-start | bytes 98308
  546.1 102.8 %all-to-all-start.5 = ((f32[32,8,32,128]{3,2,1,0:T(8,128)}), f32[32,8,32,128]{3,2,1,0:T(8,128)}, u32[]{:S(2)}, u32[]{:S(2)}) async-start(f32[32,8,32,128]{3,2,1,0:T(8,128)} %copy.19), calls=%async_computation.5 | async-start | bytes 8388608 | tf_op jit(solution)/shard_map/all_to_all | solution.py:85
Sparse Core Ops, SparseCore 0:
  225.0 242.5 all-reduce.1
where the time goes:
time: 702 us; the launch traced here: 701 us
  waiting for transfers between devices  325 us (46%)
  local copies, waits for them, and re-layouts  171 us (24%)
  blocking collectives  113 us (16%)
  other arithmetic  54.8 us (8%)
  between operations  14.4 us (2%)
  matrix products  12 us (2%)
  starting transfers between devices  10.4 us (1%)
    psum x1, waiting for transfers between devices, on_device(): gramian = lax.psum(local_gram, ('rows', 'grp'))  179 us
    all_to_all x1, waiting for transfers between devices, on_device(): lax.all_to_all(lax.all_to_all(partials, 'grp', split_axis=1, concat_axis=...  96.5 us
    all_to_all x1, blocking collectives, on_device(): lax.all_to_all(partials, 'grp', split_axis=1, concat_axis=1, tiled=True)  53.3 us
    all_to_all x1, waiting for transfers between devices, on_device(): lax.all_to_all(lax.all_to_all(answered, 'grp', split_axis=1, concat_axis=...  49 us
    scatter-add x1, other arithmetic, on_device(): item_rhs = jnp.zeros((table_rows, embed_width), jnp.float32).at[incoming....  45.3 us
    all_to_all x1, blocking collectives, on_device(): lax.all_to_all(answered, 'grp', split_axis=1, concat_axis=1, tiled=True)  30 us
    gather x13, local copies, waits for them, and re-layouts, on_device(): jnp.searchsorted(sorted_key, jnp.arange(devices + 1, dtype=jnp.int32), si...  29 us
    gather x1, local copies, waits for them, and re-layouts, on_device(): ranks = jnp.arange(lookups, dtype=jnp.int32) - starts[sorted_key]  25.9 us
  transfers between devices with their start and end apart: 3, of which 3 were waited for; matrix products, arithmetic and copies ran while one was open for 3% of the time, Pallas kernels for 0%

commit v1 on v0

--- a/solution.py
+++ b/solution.py
@@ -20,7 +20,7 @@
     local_gram = lax.dot_general(
         item_table, item_table, (((0,), (0,)), ((), ())), preferred_element_type=jnp.float32
     )
-    gramian = lax.psum(local_gram, ("rows", "grp"))
+    gramian = lax.psum(lax.psum(local_gram, "rows"), "grp")
     positions = lax.broadcasted_iota(jnp.int32, (user_count, history_length), 1)
     live = positions < counts[:, None]
     weights = live.astype(jnp.float32)

time: 702 us -> 668 us (0.952)
  waiting for transfers between devices: 325 us -> 286 us
    all_to_all x1, waiting for transfers between devices: 49 us -> 0.01 us  [on_device(): lax.all_to_all(lax.all_to_all(answered, 'grp', split_axis=1, concat_axis=...]
    psum x1 -> x2, waiting for transfers between devices: 179 us -> 190 us  [on_device(): gramian = lax.psum(lax.psum(local_gram, 'rows'), 'grp')]
  transfers between devices with their start and end apart: 3 -> 4, of which waited for: 3 -> 3; matrix products, arithmetic and copies ran while one was open for 3% -> 3% of each run, Pallas kernels for 0% -> 0%
where the time goes in v1:
time: 668 us; the launch traced here: 667 us
  waiting for transfers between devices  286 us (43%)
  local copies, waits for them, and re-layouts  171 us (26%)
  blocking collectives  114 us (17%)
  other arithmetic  54.8 us (8%)
  between operations  14.4 us (2%)
  starting transfers between devices  14.2 us (2%)
  matrix products  12 us (2%)
    psum x2, waiting for transfers between devices, on_device(): gramian = lax.psum(lax.psum(local_gram, 'rows'), 'grp')  190 us
    all_to_all x1, waiting for transfers between devices, on_device(): lax.all_to_all(lax.all_to_all(partials, 'grp', split_axis=1, concat_axis=...  96.5 us
    all_to_all x1, blocking collectives, on_device(): lax.all_to_all(partials, 'grp', split_axis=1, concat_axis=1, tiled=True)  54 us
    scatter-add x1, other arithmetic, on_device(): item_rhs = jnp.zeros((table_rows, embed_width), jnp.float32).at[incoming....  45.3 us
    all_to_all x1, blocking collectives, on_device(): lax.all_to_all(answered, 'grp', split_axis=1, concat_axis=1, tiled=True)  30 us
    gather x13, local copies, waits for them, and re-layouts, on_device(): jnp.searchsorted(sorted_key, jnp.arange(devices + 1, dtype=jnp.int32), si...  29 us
    gather x1, local copies, waits for them, and re-layouts, on_device(): ranks = jnp.arange(lookups, dtype=jnp.int32) - starts[sorted_key]  25.9 us
    gather x2, local copies, waits for them, and re-layouts, on_device(): answered = item_table[jnp.minimum(incoming, table_rows - 1)]  24.5 us
  transfers between devices with their start and end apart: 4, of which 3 were waited for; matrix products, arithmetic and copies ran while one was open for 3% of the time, Pallas kernels for 0%

profile of v1, /device:TPU:2, one launch (start us, length us, event | category | flops | bytes accessed | tf_op | source)
XLA Modules:
  0.0 667.4 jit_solution(8630922030048015869)
XLA Ops:
  8.9 5.8 sort.17
  14.7 23.0 %gather_fusion.1 = s32[4096]{0:T(1024)S(1)} fusion(s32[4096]{0:T(1024)S(1)} %get-tuple-element.108, s32[4096]{0:T(1024)S(1)} %get-tuple-element.109), kind=kCustom, calls=%fused_computation.1 | custom fusion | bytes 49152 | tf_op jit(solution)/shard_map/gather | solution.py:32
  37.8 30.3 %while.24 = (s32[]{:T(128)}, u32[257]{0:T(512)S(1)}, u32[257]{0:T(512)S(1)}, s32[4096]{0:T(1024)S(1)}, s32[]{:T(128)}, /*index=5*/s32[]{:T(128)}, s32[]{}) while((s32[]{:T(128)}, u32[257]{0:T(512)S(1)}, u32[257]{0:T(512)S(1)}, s32[4096]{0:T(1024)S(1)}, s32[]{:T(128)}, /*index=5*/s32[]{:T(128)}, s32[]{}) %tuple.47), condition=%wide.region_2.3_spmd.clone, body=%wide.region_1.0_spmd.clone.sunk | while | flops 5654 | bytes 21159 | solution.py:33
  37.8 2.2 gather_fusion
  40.1 2.2 gather_fusion
  44.8 2.2 gather_fusion
  47.1 2.2 gather_fusion
  49.4 2.2 gather_fusion
  51.8 2.2 gather_fusion
  54.1 2.2 gather_fusion
  56.4 2.2 gather_fusion
  58.7 2.2 gather_fusion
  61.1 2.2 gather_fusion
  63.4 2.2 gather_fusion
  68.1 25.9 %gather_fusion.2 = s32[4096]{0:T(1024)S(1)} fusion(s32[257]{0:T(512)S(1)} %convert_element_type.36, s32[4096]{0:T(1024)S(1)} %broadcast_clamp_fusion.1), kind=kCustom, calls=%fused_computation.2 | custom fusion | bytes 49152 | tf_op jit(solution)/shard_map/gather | solution.py:34
  94.0 15.5 %scatter_custom_fusion = s32[4096]{0:T(1024)S(1)} fusion(s32[4096]{0:T(1024)S(1)} %get-tuple-element.110, s32[4096]{0:T(1024)S(1)} %add_select_fusion.1, s32[]{:T(128)} %constant.59.clone.1), kind=kCustom, calls=%fused_computation.85 | custom fusion | bytes 16388 | tf_op jit(solution)/shard_map/scatter | solution.py:36
  109.5 15.5 %scatter_custom_fusion.1 = s32[8192]{0:T(1024)S(1)} fusion(s32[4096]{0:T(1024)S(1)} %get-tuple-element.106, s32[4096]{0:T(1024)S(1)} %get-tuple-element.107, s32[]{:T(128)} %constant.58.clone.1), kind=kCustom, calls=%fused_computation.79 | custom fusion | bytes 32772 | tf_op jit(solution)/shard_map/scatter | solution.py:38
  125.3 8.6 %all_to_all.30 = s32[8,1,1024]{2,1,0:T(1,128)S(1)} all-to-all(s32[8,1,1024]{2,1,0:T(1,128)S(1)} %reshape.212), channel_id=1, replica_groups=mesh['rows'=32,'grp'=8] {'grp'}, dimensions={0} | all-to-all | bytes 65536 | tf_op jit(solution)/shard_map/all_to_all | solution.py:42
  135.5 21.2 %all_to_all.31 = s32[32,1,256]{2,1,0:T(1,128)S(1)} all-to-all(s32[32,1,256]{2,1,0:T(1,128)S(1)} %reshape.214), channel_id=1, replica_groups=mesh['rows'=32,'grp'=8] {'rows'}, dimensions={0} | all-to-all | bytes 65536 | tf_op jit(solution)/shard_map/all_to_all | solution.py:41
  157.7 24.0 %gather_fusion.3 = bf16[8192,128]{1,0:T(8,128)(2,1)S(1)} fusion(bf16[1984,128]{1,0:T(8,128)(2,1)S(1)} %copy-done, s32[8192]{0:T(1024)S(1)} %broadcast_clamp_fusion), kind=kCustom, calls=%fused_computation.3 | custom fusion | bytes 4227072 | tf_op jit(solution)/shard_map/gather | solution.py:48
  182.2 30.0 %all_to_all.32 = bf16[32,8,32,128]{3,2,0,1:T(8,128)(2,1)S(1)} all-to-all(bf16[32,8,32,128]{3,2,0,1:T(8,128)(2,1)S(1)} %copy.16), channel_id=1, replica_groups=mesh['rows'=32,'grp'=8] {'grp'}, dimensions={1} | all-to-all | bytes 4194304 | tf_op jit(solution)/shard_map/all_to_all | solution.py:50
  214.1 4.0 all-to-all-start.3
  219.4 147.8 %all-reduce.3.cloned.1.call-done = f32[128,128]{1,0:T(8,128)} async-done(((f32[128,128]{1,0:T(8,128)}), f32[128,128]{1,0:T(8,128)}) %all-reduce.3.cloned.1.call-update) | async-done | bytes 65552 | tf_op jit(solution)/shard_map/psum | solution.py:23
  367.3 14.9 %gather_fusion.4 = bf16[4096,128]{1,0:T(8,128)(2,1)} fusion(bf16[8192,128]{1,0:T(8,128)(2,1)S(1)} %bitcast.60, s32[4096]{0:T(1024)S(1)} %get-tuple-element.105), kind=kCustom, calls=%fused_computation.4 | custom fusion | bytes 2113536 | tf_op jit(solution)/shard_map/gather | solution.py:57
  387.4 42.0 %all-reduce.5.cloned.1.call-done = f32[128,128]{1,0:T(8,128)} async-done(((f32[128,128]{1,0:T(8,128)}), f32[128,128]{1,0:T(8,128)}) %all-reduce.5.cloned.1.call-update) | async-done | bytes 65552 | tf_op jit(solution)/shard_map/psum | solution.py:23
  436.5 12.8 %scatter_custom_fusion.2 = f32[8192,128]{1,0:T(8,128)} fusion(s32[4096]{0:T(1024)S(1)} %get-tuple-element.106, f32[4096,128]{1,0:T(8,128)S(1)} %bitcast.63, f32[]{:T(128)} %constant.71.clone.1), kind=kCustom, calls=%fused_computation.15 | custom fusion | bytes 4194308 | tf_op jit(solution)/shard_map/scatter | solution.py:82
  449.2 2.8 copy.18
  452.0 54.0 %all_to_all.33 = f32[32,8,32,128]{3,2,0,1:T(8,128)S(1)} all-to-all(f32[32,8,32,128]{3,2,0,1:T(8,128)S(1)} %copy.18), channel_id=1, replica_groups=mesh['rows'=32,'grp'=8] {'grp'}, dimensions={1} | all-to-all | bytes 8388608 | tf_op jit(solution)/shard_map/all_to_all | solution.py:86
  506.1 2.6 copy.19
  508.7 10.0 %all-to-all-start.5 = ((f32[32,8,32,128]{3,2,1,0:T(8,128)}), f32[32,8,32,128]{3,2,1,0:T(8,128)}, u32[]{:S(2)}, u32[]{:S(2)}) async-start(f32[32,8,32,128]{3,2,1,0:T(8,128)} %copy.19), calls=%async_computation.5 | async-start | bytes 8388608 | tf_op jit(solution)/shard_map/all_to_all | solution.py:85
  518.8 96.5 %all-to-all-done.5 = f32[32,8,32,128]{3,2,1,0:T(8,128)} async-done(((f32[32,8,32,128]{3,2,1,0:T(8,128)}), f32[32,8,32,128]{3,2,1,0:T(8,128)}, u32[]{:S(2)}, u32[]{:S(2)}) %all-to-all-start.5) | async-done | bytes 4194336 | tf_op jit(solution)/shard_map/all_to_all | solution.py:85
  615.3 45.3 %scatter_custom_fusion.3 = f32[1984,128]{1,0:T(8,128)} fusion(s32[8192]{0:T(1024)S(1)} %bitcast.84, f32[8192,128]{1,0:T(8,128)} %bitcast.29, f32[]{:T(128)} %constant.71.clone.1), kind=kCustom, calls=%fused_computation.28 | custom fusion | flops 1048576 | bytes 1016320 | tf_op jit(solution)/shard_map/scatter-add | solution.py:95
  (138 shorter events, 25.5 us)
Async XLA Ops:
  7.2 150.5 %copy-start = (bf16[1984,128]{1,0:T(8,128)(2,1)S(1)}, bf16[1984,128]{1,0:T(8,128)(2,1)}, u32[]{:S(2)}) copy-start(bf16[1984,128]{1,0:T(8,128)(2,1)} %param.5) | copy-start | bytes 1523716
  214.1 153.1 %all-to-all-start.3 = ((bf16[32,8,32,128]{3,2,1,0:T(8,128)(2,1)}), bf16[32,8,32,128]{3,2,1,0:T(8,128)(2,1)S(1)}, u32[]{:S(2)}, u32[]{:S(2)}) async-start(bf16[32,8,32,128]{3,2,1,0:T(8,128)(2,1)} %copy.17), calls=%async_computation.3 | async-start | bytes 4194304 | tf_op jit(solution)/shard_map/all_to_all | solution.py:49
  218.1 149.1 %all-reduce.3.cloned.1.call-start = ((), (), s32[]{:S(2)}) async-start(), calls=%async_computation.6 | async-start | bytes 131072 | tf_op jit(solution)/shard_map/psum | solution.py:23
  219.2 210.3 %all-reduce.5.cloned.1.call-start = ((), (), s32[]{:S(2)}) async-start(), calls=%async_computation.7 | async-start | bytes 131072 | tf_op jit(solution)/shard_map/psum | solution.py:23
  367.2 18.5 %copy-start.4 = (s32[64]{0:T(128)S(1)}, s32[64]{0:T(128)}, u32[]{:S(2)}) copy-start(s32[64]{0:T(128)} %param.7) | copy-start | bytes 772
  382.2 50.8 %copy-start.1 = (bf16[4096,128]{1,0:T(8,128)(2,1)S(1)}, bf16[4096,128]{1,0:T(8,128)(2,1)}, u32[]{:S(2)}) copy-start(bf16[4096,128]{1,0:T(8,128)(2,1)} %gather_fusion.4) | copy-start | bytes 3145732
  429.4 6.4 copy-start.2
  436.3 15.7 %copy-start.3 = (f32[64,128]{1,0:T(8,128)}, f32[64,128]{1,0:T(8,128)S(1)}, u32[]{:S(2)}) copy-start(f32[64,128]{1,0:T(8,128)S(1)} %multiply_add_fusion) | copy-start | bytes 98308
  508.7 106.6 %all-to-all-start.5 = ((f32[32,8,32,128]{3,2,1,0:T(8,128)}), f32[32,8,32,128]{3,2,1,0:T(8,128)}, u32[]{:S(2)}, u32[]{:S(2)}) async-start(f32[32,8,32,128]{3,2,1,0:T(8,128)} %copy.19), calls=%async_computation.5 | async-start | bytes 8388608 | tf_op jit(solution)/shard_map/all_to_all | solution.py:85
Sparse Core Ops, SparseCore 0:
  223.0 144.1 all-reduce.2
  369.5 59.8 all-reduce.4
